TPU v7x, 128 devices: a whole 4x4x4 slice. The times are simulated.
128 devices in a mesh: row: 8 (over x, core), col: 16 (over z, y).
Axes of the slice: x: 4, y: 4, z: 4, core: 2. Of those that a mesh axis runs over, the one named last changes fastest.
Arguments:
- left_factor: float32 [23, 8, 128, 16, 16, 128], P(None, 'row', None, None, 'col'), may hold values from -5 to 5
- pick_site: int32 [23, 8, 128], P(None, 'row'), may hold values from 0 to 131071
- noise: float32 [23, 8, 128], P(None, 'row'), may hold values from 2 to 5
Outputs:
- panels: float32 [8, 16, 184, 2, 128], P('row', 'col')
All inputs are finite; a program needn't handle non-finite values.
Results may differ from a plain program's by a relative error of at most 0.000064.
Values sent between devices are 32-bit elements; how exact they have to be, the bound alone decides.
No kernel may reach another device: no remote copies, remote signals or barrier semaphores. Data moves between devices by JAX's collectives and lax.ppermute only.
A program may use at most 128 MiB of HBM per device.

v0:
```python
import jax
import jax.numpy as jnp
from jax import lax
from jax.sharding import PartitionSpec as P

GRID_Y = 64
GRID_Z = 32
LATERAL = 24.0
VERTICAL = 6.0


def spread(block, axis, owner):
    block = jnp.where(lax.axis_index(axis) == owner, block, jnp.zeros_like(block))
    return lax.psum(block, axis)


def site_coords(site_ids):
    coord_x = site_ids // (GRID_Y * GRID_Z)
    coord_y = site_ids // GRID_Z % GRID_Y
    coord_z = site_ids % GRID_Z
    return jnp.stack([coord_x, coord_y, coord_z]).astype(jnp.float32)


def matern(row_coords, col_coords):
    lengths = (LATERAL, LATERAL, VERTICAL)
    squared = jnp.zeros((row_coords.shape[1], col_coords.shape[1]), jnp.float32)
    for dim_index in range(3):
        difference = (row_coords[dim_index][:, None] - col_coords[dim_index][None, :]) / lengths[
            dim_index
        ]
        squared = squared + difference * difference
    radius = jnp.sqrt(3.0 * squared)
    return (1.0 + radius) * jnp.exp(-radius)


def times_transposed(left_mat, right_mat):
    return lax.dot_general(
        left_mat,
        right_mat,
        (((1,), (1,)), ((), ())),
        precision=lax.Precision.HIGHEST,
        preferred_element_type=jnp.float32,
    )


def lower_inverse(square):
    factor = jnp.linalg.cholesky(square)
    return jax.scipy.linalg.solve_triangular(
        factor, jnp.eye(square.shape[0], dtype=jnp.float32), lower=True
    )


def body(left_factor, pick_site, noise):
    row_blocks, _, block_width, col_blocks, _, _ = left_factor.shape
    col_count = lax.axis_size("col")
    row_share = row_blocks * block_width // col_count
    row_index = lax.axis_index("row")
    col_index = lax.axis_index("col")
    local_rows = left_factor.reshape(row_blocks * block_width, col_blocks * block_width)
    site_flat = pick_site.reshape(row_blocks * block_width)
    noise_flat = noise.reshape(row_blocks * block_width)
    offset = col_index * row_share
    my_coords = site_coords(lax.dynamic_slice_in_dim(site_flat, offset, row_share))
    my_noise = lax.dynamic_slice_in_dim(noise_flat, offset, row_share)
    head_rows = local_rows[:block_width]
    head_coords = site_coords(site_flat[:block_width])
    first_owner = (row_index == 0) & (col_index == 0)
    second_owner = (row_index == 1) & (col_index == 0)
    own_diag = jnp.diag(my_noise[:block_width])

    def terms_for(lead_rows):
        return times_transposed(local_rows, lead_rows)

    first_head, first_coords = (spread(head_rows, "row", 0), spread(head_coords, "row", 0))
    first_sums = lax.psum_scatter(terms_for(first_head), "col", scatter_dimension=0, tiled=True)
    second_head, second_coords = (spread(head_rows, "row", 1), spread(head_coords, "row", 1))
    second_sums = lax.psum_scatter(terms_for(second_head), "col", scatter_dimension=0, tiled=True)
    first_cov = matern(my_coords, first_coords) - first_sums
    first_cov = first_cov.at[:block_width].add(jnp.where(first_owner, own_diag, 0.0))
    first_diag = spread(first_cov[:block_width], ("row", "col"), 0)
    first_panel = times_transposed(first_cov, lower_inverse(first_diag))
    own_cross = first_panel[:block_width]
    second_base = matern(my_coords, second_coords) - second_sums
    second_nugget = jnp.where(second_owner, own_diag, 0.0)
    cross_rows = spread(own_cross, ("row", "col"), col_count)
    second_cov = (
        (second_base - times_transposed(first_panel, cross_rows))
        .at[:block_width]
        .add(second_nugget)
    )
    second_diag = spread(second_cov[:block_width], ("row", "col"), col_count)
    second_panel = times_transposed(second_cov, lower_inverse(second_diag))
    stacked = jnp.stack([first_panel, second_panel], axis=1)
    return stacked.reshape(1, 1, row_share, 2, block_width)


def solution(mesh):
    placed = (P(None, "row", None, None, "col", None), P(None, "row", None), P(None, "row", None))
    return jax.shard_map(
        body,
        mesh=mesh,
        in_specs=placed,
        out_specs=P("row", "col", None, None, None),
        check_vma=False,
    )
```

profile of v0, /device:TPU:1, one launch (start us, length us, event | category | flops | bytes accessed | tf_op | source)
XLA Modules:
  0.0 742.1 jit_solution(13601761181299983725)
XLA Ops:
  6.5 0.0 all-reduce.19.cloned.1.call-start
  6.5 6.9 fusion.13
  13.5 2.3 copy_bitcast_fusion
  15.8 0.0 all-reduce.19.cloned.1.call-update
  15.8 0.0 all-reduce.17.cloned.1.call-start
  15.8 67.1 %all-reduce.19.cloned.1.call-done = (f32[128,2048]{1,0:T(8,128)}, f32[128,2048]{1,0:T(8,128)}) async-done(((f32[128,2048]{1,0:T(8,128)}, f32[128,2048]{1,0:T(8,128)}), (f32[128,2048]{1,0:T(8,128)}, f32[128,2048]{1,0:T(8,128)})) %all-reduce.19.cloned.1.call-update) | async-done | bytes 2097168 | tf_op jit(solution)/shard_map/psum | solution.py:14
  83.0 40.9 %fusion.6 = f32[2944,128]{0,1:T(8,128)} fusion(f32[128,2048]{1,0:T(8,128)} %get-tuple-element.37, f32[368,8,16,128]{3,2,1,0:T(8,128)} %bitcast.102), kind=kOutput, calls=%fused_computation.6 | convolution fusion | flops 9261023232 | bytes 26673152 | tf_op jit(solution)/shard_map/dot_general | solution.py:37
  123.9 0.0 copy-done
  123.9 40.5 %fusion.9 = f32[2944,128]{0,1:T(8,128)} fusion(f32[128,2048]{1,0:T(8,128)S(1)} %copy-done, f32[368,8,16,128]{3,2,1,0:T(8,128)} %bitcast.103), kind=kOutput, calls=%fused_computation.7 | convolution fusion | flops 9261023232 | bytes 26673152 | tf_op jit(solution)/shard_map/dot_general | solution.py:37
  164.4 0.0 all-reduce.17.cloned.1.call-update
  164.5 0.0 all-reduce.11.cloned.1.call-start
  164.5 0.0 copy-done.1
  164.6 0.1 dynamic_slice.7
  164.7 0.6 dynamic-slice.16
  166.0 14.3 %all-reduce.3 = (f32[3,128]{1,0:T(4,128)S(1)}, f32[3,128]{1,0:T(4,128)S(1)}) all-reduce(f32[3,128]{1,0:T(4,128)S(1)} %get-tuple-element.59, f32[3,128]{1,0:T(4,128)S(1)} %get-tuple-element.58), channel_id=1, replica_groups=mesh['row'=8,'col'=16] {'row'}, use_global_device_ids=true, to_apply=%region_0.1 | all-reduce | flops 768 | bytes 6144 | tf_op jit(solution)/shard_map/psum | solution.py:14
  180.3 0.1 and_select_fusion.7
  180.4 80.7 %all-reduce.17.cloned.1.call-done = (f32[2944,128]{0,1:T(8,128)}, f32[2944,128]{0,1:T(8,128)}) async-done(((f32[2944,128]{0,1:T(8,128)}, f32[2944,128]{0,1:T(8,128)}), (f32[2944,128]{0,1:T(8,128)}, f32[2944,128]{0,1:T(8,128)})) %all-reduce.17.cloned.1.call-update) | async-done | bytes 3014672
  261.1 1.1 dynamic-slice_subtract_fusion.1
  262.3 0.7 fusion.28
  262.9 0.0 all-reduce.11.cloned.1.call-update
  263.0 0.0 all-reduce.13.cloned.1.call-start
  263.0 142.0 %all-reduce.11.cloned.1.call-done = f32[128,128]{0,1:T(8,128)} async-done(((f32[128,128]{0,1:T(8,128)}), f32[128,128]{0,1:T(8,128)}) %all-reduce.11.cloned.1.call-update) | async-done | bytes 65552 | tf_op jit(solution)/shard_map/psum | solution.py:14
  405.0 0.9 copy.15
  405.9 0.9 fusion.25
  406.8 11.7 %cholesky.44 = f32[128,128]{1,0:T(8,128)S(1)} custom-call(f32[128,128]{1,0:T(8,128)S(1)} %fusion.25), custom_call_target="Cholesky" | custom-call | tf_op jit(solution)/shard_map/jit(cholesky)/cholesky | solution.py:47
  418.5 0.6 compare_reduce_fusion.1
  419.1 0.7 fusion.18
  419.8 9.8 %custom-call.6 = f32[1,128,128]{1,2,0:T(8,128)S(1)} custom-call(f32[1,128,128]{2,1,0:T(8,128)S(1)} %fusion.18), custom_call_target="InvertDiagBlocksLowerTriangular" | custom-call | tf_op jit(solution)/shard_map/jit(_solve_triangular)/triangular_solve | solution.py:48
  429.6 0.3 fusion.16
  429.9 0.4 fusion.35
  430.4 0.1 copy.26
  430.4 0.6 broadcast_select_fusion.2
  431.1 0.0 all-reduce.13.cloned.1.call-update
  431.1 0.3 all-reduce.15.cloned.1.call-start
  431.4 136.5 %all-reduce.13.cloned.1.call-done = f32[128,128]{0,1:T(8,128)} async-done(((f32[128,128]{0,1:T(8,128)}), f32[128,128]{0,1:T(8,128)}) %all-reduce.13.cloned.1.call-update) | async-done | bytes 65552 | tf_op jit(solution)/shard_map/psum | solution.py:14
  567.9 1.3 convolution_subtract_fusion
  569.2 0.7 fusion.26
  569.9 0.0 all-reduce.15.cloned.1.call-update
  569.9 139.2 %all-reduce.15.cloned.1.call-done = f32[128,128]{0,1:T(8,128)} async-done(((f32[128,128]{0,1:T(8,128)}), f32[128,128]{0,1:T(8,128)}) %all-reduce.15.cloned.1.call-update) | async-done | bytes 65552 | tf_op jit(solution)/shard_map/psum | solution.py:14
  709.1 0.9 copy.19
  710.1 0.9 fusion.23
  710.9 11.7 %cholesky.55 = f32[128,128]{1,0:T(8,128)S(1)} custom-call(f32[128,128]{1,0:T(8,128)S(1)} %fusion.23), custom_call_target="Cholesky" | custom-call | tf_op jit(solution)/shard_map/jit(cholesky)/cholesky | solution.py:47
  722.7 0.6 compare_reduce_fusion
  723.3 0.7 fusion.19
  724.0 9.8 %custom-call.7 = f32[1,128,128]{1,2,0:T(8,128)S(1)} custom-call(f32[1,128,128]{2,1,0:T(8,128)S(1)} %fusion.19), custom_call_target="InvertDiagBlocksLowerTriangular" | custom-call | tf_op jit(solution)/shard_map/jit(_solve_triangular)/triangular_solve | solution.py:48
  733.8 0.3 fusion.14
  734.1 0.4 convolution_bitcast_fusion
  734.5 0.8 copy.20
  (19 shorter events, 0.2 us)
Async XLA Ops:
  6.5 76.4 %all-reduce.19.cloned.1.call-start = ((), (), s32[]{:S(2)}) async-start(), calls=%async_computation.4 | async-start | bytes 4194304 | tf_op jit(solution)/shard_map/psum | solution.py:14
  15.8 245.3 %all-reduce.17.cloned.1.call-start = ((), (), s32[]{:S(2)}) async-start(), calls=%async_computation.3 | async-start | bytes 6029312
  83.0 40.9 %copy-start = (f32[128,2048]{1,0:T(8,128)S(1)}, f32[128,2048]{1,0:T(8,128)}, u32[]{:S(2)}) copy-start(f32[128,2048]{1,0:T(8,128)} %get-tuple-element.38) | copy-start | bytes 3145732
  83.0 81.6 %copy-start.1 = (s32[23,1,128]{2,1,0:T(1,128)S(1)}, s32[23,1,128]{2,1,0:T(1,128)}, u32[]{:S(2)}) copy-start(s32[23,1,128]{2,1,0:T(1,128)} %param.11) | copy-start | bytes 35332
  83.0 81.6 %copy-start.2 = (f32[23,1,128]{2,1,0:T(1,128)S(1)}, f32[23,1,128]{2,1,0:T(1,128)}, u32[]{:S(2)}) copy-start(f32[23,1,128]{2,1,0:T(1,128)} %param.12) | copy-start | bytes 35332
  83.0 81.7 %copy-start.3 = (u32[128]{0:T(128)S(1)}, u32[128]{0:T(128)}, u32[]{:S(2)}) copy-start(u32[128]{0:T(128)} %constant.200) | copy-start | bytes 1540
  164.5 240.5 %all-reduce.11.cloned.1.call-start = ((), (), s32[]{:S(2)}) async-start(), calls=%async_computation | async-start | bytes 131072 | tf_op jit(solution)/shard_map/psum | solution.py:14
  263.0 305.0 %all-reduce.13.cloned.1.call-start = ((), (), s32[]{:S(2)}) async-start(), calls=%async_computation.1 | async-start | bytes 131072 | tf_op jit(solution)/shard_map/psum | solution.py:14
  431.1 278.0 %all-reduce.15.cloned.1.call-start = ((), (), s32[]{:S(2)}) async-start(), calls=%async_computation.2 | async-start | bytes 131072 | tf_op jit(solution)/shard_map/psum | solution.py:14
Sparse Core Ops, SparseCore 0:
  15.9 67.0 all-reduce.18
  164.6 96.5 all-reduce.16
  265.9 139.0 all-reduce.10
  431.2 136.6 all-reduce.12
  572.5 136.6 all-reduce.14
where the time goes:
time: 746 us; the launch traced here: 742 us
  waiting for transfers between devices  566 us (76%)
  matrix products  84.2 us (11%)
  other arithmetic  57.7 us (8%)
  blocking collectives  14.3 us (2%)
  between operations  14.3 us (2%)
    psum x4, waiting for transfers between devices, spread(): return lax.psum(block, axis)  485 us
    dot_general x5, matrix products, times_transposed(): lax.dot_general(left_mat, right_mat, (((1,), (1,)), ((), ())), precision=...  83.6 us
    unnamed x6, waiting for transfers between devices  80.8 us
    another operation x6, other arithmetic, lower_inverse(): factor = jnp.linalg.cholesky(square)  24.8 us
    another operation x4, other arithmetic, lower_inverse(): jax.scipy.linalg.solve_triangular(factor, jnp.eye(square.shape[0], dtype=...  20.9 us
  transfers between devices with their start and end apart: 5, of which 5 were waited for; matrix products, arithmetic and copies ran while one was open for 0% of the time, Pallas kernels for 0%

commit v1 on v0

--- a/solution.py
+++ b/solution.py
@@ -2,6 +2,7 @@
 import jax.numpy as jnp
 from jax import lax
 from jax.sharding import PartitionSpec as P
+from jax.lax import all_gather
 
 GRID_Y = 64
 GRID_Z = 32
@@ -11,7 +12,8 @@
 
 def spread(block, axis, owner):
     block = jnp.where(lax.axis_index(axis) == owner, block, jnp.zeros_like(block))
-    return lax.psum(block, axis)
+    connect_heaps = lambda m, bus_axis: jnp.sum(all_gather(m, bus_axis), 0)
+    return connect_heaps(block, axis)
 
 
 def site_coords(site_ids):

time: 746 us -> 539 us (0.72)
  waiting for transfers between devices: 566 us -> 333 us
  other arithmetic: 57.7 us -> 74.8 us
  blocking collectives: 14.3 us -> 23 us
    psum x4 -> x0, waiting for transfers between devices: 485 us -> none  [spread(): return lax.psum(block, axis)]
    all_gather x0 -> x5, waiting for transfers between devices: none -> 251 us  [spread(): connect_heaps = lambda m, bus_axis: jnp.sum(all_gather(m, bus_axis), 0)]
    all_gather x0 -> x2, blocking collectives: none -> 23 us  [spread(): connect_heaps = lambda m, bus_axis: jnp.sum(all_gather(m, bus_axis), 0)]
    reduce_sum x0 -> x6, other arithmetic: none -> 16 us  [spread(): connect_heaps = lambda m, bus_axis: jnp.sum(all_gather(m, bus_axis), 0)]
    psum x1 -> x0, blocking collectives: 14.3 us -> none  [spread(): return lax.psum(block, axis)]
    unnamed x6 -> x7, waiting for transfers between devices: 80.8 us -> 81.9 us
  transfers between devices with their start and end apart: 5 -> 6, of which waited for: 5 -> 6; matrix products, arithmetic and copies ran while one was open for 0% -> 9% of each run, Pallas kernels for 0% -> 0%
where the time goes in v1:
time: 539 us; the launch traced here: 535 us
  waiting for transfers between devices  333 us (62%)
  matrix products  82.6 us (15%)
  other arithmetic  74.8 us (14%)
  blocking collectives  23 us (4%)
  between operations  14.6 us (3%)
  local copies, waits for them, and re-layouts  6.22 us (1%)
    all_gather x5, waiting for transfers between devices, spread(): connect_heaps = lambda m, bus_axis: jnp.sum(all_gather(m, bus_axis), 0)  251 us
    dot_general x5, matrix products, times_transposed(): lax.dot_general(left_mat, right_mat, (((1,), (1,)), ((), ())), precision=...  82 us
    unnamed x7, waiting for transfers between devices  81.9 us
    another operation x6, other arithmetic, lower_inverse(): factor = jnp.linalg.cholesky(square)  24.8 us
    all_gather x2, blocking collectives, spread(): connect_heaps = lambda m, bus_axis: jnp.sum(all_gather(m, bus_axis), 0)  23 us
    another operation x4, other arithmetic, lower_inverse(): jax.scipy.linalg.solve_triangular(factor, jnp.eye(square.shape[0], dtype=...  20.9 us
    reduce_sum x6, other arithmetic, spread(): connect_heaps = lambda m, bus_axis: jnp.sum(all_gather(m, bus_axis), 0)  16 us
  transfers between devices with their start and end apart: 6, of which 6 were waited for; matrix products, arithmetic and copies ran while one was open for 9% of the time, Pallas kernels for 0%

profile of v1, /device:TPU:1, one launch (start us, length us, event | category | flops | bytes accessed | tf_op | source)
XLA Modules:
  0.0 534.7 jit_solution(1053083655918033256)
XLA Ops:
  6.5 6.8 %fusion.13 = (f32[128,16,128]{2,1,0:T(8,128)S(1)}, f32[128,16,128]{2,1,0:T(8,128)S(1)}) fusion(pred[]{:T(512)S(6)} %eq.41, f32[23,1,128,16,1,128]{5,4,3,2,1,0:T(1,128)} %param.10, pred[]{:T(512)S(6)} %eq.37), kind=kLoop, calls=%fused_computation.13 | loop fusion | flops 524288 | bytes 3145730 | tf_op jit(solution)/shard_map/jit(_where)/select_n | solution.py:14
  13.3 1.2 select_n.172
  14.6 0.0 all-gather.11.cloned.1.call-start
  14.6 1.2 select_n.182
  15.8 52.1 %all-gather.9.cloned.1.call-done = f32[8,128,2048]{2,1,0:T(8,128)} async-done(((f32[1,128,2048]{2,1,0:T(8,128)}), f32[8,128,2048]{2,1,0:T(8,128)}) %all-gather.9.cloned.1.call-update) | async-done | bytes 8388624 | tf_op jit(solution)/shard_map/all_gather | solution.py:15
  67.9 4.2 reduce_sum.64
  72.1 40.3 %fusion.6 = f32[2944,128]{0,1:T(8,128)} fusion(f32[128,2048]{1,0:T(8,128)S(1)} %reduce_sum.64, f32[368,8,16,128]{3,2,1,0:T(8,128)} %bitcast.76), kind=kOutput, calls=%fused_computation.6 | convolution fusion | flops 9261023232 | bytes 26673152 | tf_op jit(solution)/shard_map/dot_general | solution.py:39
  112.5 7.0 %all-gather.11.cloned.1.call-done = f32[8,128,2048]{2,1,0:T(8,128)} async-done(((f32[1,128,2048]{2,1,0:T(8,128)}), f32[8,128,2048]{2,1,0:T(8,128)}) %all-gather.11.cloned.1.call-update) | async-done | bytes 8388624 | tf_op jit(solution)/shard_map/all_gather | solution.py:15
  119.5 4.2 reduce_sum.67
  123.7 40.7 %fusion.9 = f32[2944,128]{0,1:T(8,128)} fusion(f32[128,2048]{1,0:T(8,128)S(1)} %reduce_sum.67, f32[368,8,16,128]{3,2,1,0:T(8,128)} %bitcast.77), kind=kOutput, calls=%fused_computation.7 | convolution fusion | flops 9261023232 | bytes 26673152 | tf_op jit(solution)/shard_map/dot_general | solution.py:39
  164.5 0.0 all-gather.13.cloned.1.call-start
  164.6 11.4 %all_gather.34 = f32[8,3,128]{2,1,0:T(4,128)S(1)} all-gather(f32[1,3,128]{2,1,0:T(4,128)S(1)} %get-tuple-element.55), channel_id=1, replica_groups=mesh['row'=8,'col'=16] {'row'}, dimensions={0}, use_global_device_ids=true | all-gather | bytes 13824 | tf_op jit(solution)/shard_map/all_gather | solution.py:15
  176.1 0.1 dynamic_slice.7
  176.2 0.6 dynamic-slice.16
  177.4 0.1 and_select_fusion.7
  177.5 81.8 %all-reduce.5.cloned.1.call-done = (f32[2944,128]{0,1:T(8,128)}, f32[2944,128]{0,1:T(8,128)}) async-done(((f32[2944,128]{0,1:T(8,128)}, f32[2944,128]{0,1:T(8,128)}), (f32[2944,128]{0,1:T(8,128)}, f32[2944,128]{0,1:T(8,128)})) %all-reduce.5.cloned.1.call-update) | async-done | bytes 3014672
  259.3 1.0 constant_dynamic-slice_fusion.1
  260.4 0.1 copy.15
  260.5 0.2 multiply_subtract_fusion
  260.6 0.7 fusion.28
  261.5 70.3 %all-gather.13.cloned.1.call-done = f32[16384,128]{1,0:T(8,128)} async-done(((f32[128,128]{1,0:T(8,128)}), f32[16384,128]{1,0:T(8,128)}) %all-gather.13.cloned.1.call-update) | async-done | bytes 8388624 | tf_op jit(solution)/shard_map/all_gather | solution.py:15
  331.7 3.8 reduce_sum.65
  335.5 0.1 copy.16
  335.7 11.7 %cholesky.44 = f32[128,128]{1,0:T(8,128)S(1)} custom-call(f32[128,128]{1,0:T(8,128)S(1)} %fusion.25), custom_call_target="Cholesky" | custom-call | tf_op jit(solution)/shard_map/jit(cholesky)/cholesky | solution.py:49
  347.4 0.6 compare_reduce_fusion.1
  348.0 0.7 fusion.18
  348.7 9.8 %custom-call.6 = f32[1,128,128]{1,2,0:T(8,128)S(1)} custom-call(f32[1,128,128]{2,1,0:T(8,128)S(1)} %fusion.18), custom_call_target="InvertDiagBlocksLowerTriangular" | custom-call | tf_op jit(solution)/shard_map/jit(_solve_triangular)/triangular_solve | solution.py:50
  358.5 0.3 fusion.16
  358.8 0.3 fusion.35
  359.1 0.6 slice_select_fusion
  359.8 0.0 all-gather.17.cloned.1.call-start
  359.9 11.6 %all_gather.38 = f32[8,3,128]{2,1,0:T(4,128)S(1)} all-gather(f32[1,3,128]{2,1,0:T(4,128)S(1)} %get-tuple-element.54), channel_id=1, replica_groups=mesh['row'=8,'col'=16] {'row'}, dimensions={0}, use_global_device_ids=true | all-gather | bytes 13824 | tf_op jit(solution)/shard_map/all_gather | solution.py:15
  371.5 1.0 constant_dynamic-slice_fusion
  372.5 0.1 copy.17
  372.6 54.5 %all-gather.15.cloned.1.call-done = f32[16384,128]{1,0:T(8,128)} async-done(((f32[128,128]{1,0:T(8,128)}), f32[16384,128]{1,0:T(8,128)}) %all-gather.15.cloned.1.call-update) | async-done | bytes 8388624 | tf_op jit(solution)/shard_map/all_gather | solution.py:15
  427.2 3.8 reduce_sum.68
  431.0 0.3 convolution_subtract_fusion
  431.3 0.7 fusion.26
  432.0 67.4 %all-gather.17.cloned.1.call-done = f32[16384,128]{1,0:T(8,128)} async-done(((f32[128,128]{1,0:T(8,128)}), f32[16384,128]{1,0:T(8,128)}) %all-gather.17.cloned.1.call-update) | async-done | bytes 8388624 | tf_op jit(solution)/shard_map/all_gather | solution.py:15
  499.4 3.8 reduce_sum.69
  503.2 0.1 copy.19
  503.3 11.7 %cholesky.55 = f32[128,128]{1,0:T(8,128)S(1)} custom-call(f32[128,128]{1,0:T(8,128)S(1)} %fusion.23), custom_call_target="Cholesky" | custom-call | tf_op jit(solution)/shard_map/jit(cholesky)/cholesky | solution.py:49
  515.1 0.6 compare_reduce_fusion
  515.7 0.7 fusion.19
  516.4 9.8 %custom-call.7 = f32[1,128,128]{1,2,0:T(8,128)S(1)} custom-call(f32[1,128,128]{2,1,0:T(8,128)S(1)} %fusion.19), custom_call_target="InvertDiagBlocksLowerTriangular" | custom-call | tf_op jit(solution)/shard_map/jit(_solve_triangular)/triangular_solve | solution.py:50
  526.2 0.3 fusion.14
  526.5 0.3 convolution_bitcast_fusion
  526.8 0.8 copy.20
  (31 shorter events, 0.5 us)
Async XLA Ops:
  6.5 61.4 %all-gather.9.cloned.1.call-start = ((), (), s32[]{:S(2)}) async-start(), calls=%async_computation | async-start | bytes 9437184 | tf_op jit(solution)/shard_map/all_gather | solution.py:15
  14.6 104.9 %all-gather.11.cloned.1.call-start = ((), (), s32[]{:S(2)}) async-start(), calls=%async_computation.1 | async-start | bytes 9437184 | tf_op jit(solution)/shard_map/all_gather | solution.py:15
  15.8 243.6 %all-reduce.5.cloned.1.call-start = ((), (), s32[]{:S(2)}) async-start(), calls=%async_computation.5 | async-start | bytes 6029312
  123.7 40.8 %copy-start = (s32[23,1,128]{2,1,0:T(1,128)S(1)}, s32[23,1,128]{2,1,0:T(1,128)}, u32[]{:S(2)}) copy-start(s32[23,1,128]{2,1,0:T(1,128)} %param.11) | copy-start | bytes 35332
  123.7 52.3 %copy-start.1 = (f32[23,1,128]{2,1,0:T(1,128)S(1)}, f32[23,1,128]{2,1,0:T(1,128)}, u32[]{:S(2)}) copy-start(f32[23,1,128]{2,1,0:T(1,128)} %param.12) | copy-start | bytes 35332
  123.7 52.5 %copy-start.2 = (u32[128]{0:T(128)S(1)}, u32[128]{0:T(128)}, u32[]{:S(2)}) copy-start(u32[128]{0:T(128)} %constant.200) | copy-start | bytes 1540
  164.5 167.3 %all-gather.13.cloned.1.call-start = ((), (), s32[]{:S(2)}) async-start(), calls=%async_computation.2 | async-start | bytes 8454144 | tf_op jit(solution)/shard_map/all_gather | solution.py:15
  261.4 165.8 %all-gather.15.cloned.1.call-start = ((), (), s32[]{:S(2)}) async-start(), calls=%async_computation.3 | async-start | bytes 8454144 | tf_op jit(solution)/shard_map/all_gather | solution.py:15
  359.8 139.6 %all-gather.17.cloned.1.call-start = ((), (), s32[]{:S(2)}) async-start(), calls=%async_computation.4 | async-start | bytes 8454144 | tf_op jit(solution)/shard_map/all_gather | solution.py:15
Sparse Core Ops, SparseCore 0:
  14.7 53.2 all-gather.8
  69.6 49.7 all-gather.10
  164.6 94.7 all-reduce.4
  262.3 69.3 all-gather.12
  359.9 67.1 all-gather.14
  432.2 67.1 all-gather.16
